TPU v7x, 32 devices: a whole 2x2x4 slice. The times are simulated.
32 devices in a mesh: groups: 2 (over y), tm: 16 (over z, x, core).
Axes of the slice: x: 2, y: 2, z: 4, core: 2. Of those that a mesh axis runs over, the one named last changes fastest.
Arguments:
- ref_traj: float32 [8, 1024, 256], P('groups', 'tm'), parts along dimension 0, may hold values from -6 to 6
- cost_weights: float32 [8, 1024, 256], P('groups', 'tm'), parts along dimension 0, may hold values from 0.1 to 10
- x_init: float32 [8, 256], P('groups'), parts along dimension 0, may hold values from -6 to 6
- decay: float32 [256], replicated, as said below
- coupling: float32 [3, 64, 64], replicated, may hold values from -0.00018310547 to 0.00018310547
- links: int32 [3, 2], replicated, may hold values from 0 to 3, as said below
- input_map: float32 [256, 64], replicated, may hold values from -0.0007324219 to 0.0007324219
- ff_gain: float32 [64, 256], replicated, may hold values from -0.01171875 to 0.01171875
- lengths: int32 [8, 4], P('groups'), parts along dimension 0, may hold values from 1 to 512, 1024 in all within a row
Outputs:
- states: float32 [8, 1024, 256], P('groups', 'tm'), parts along dimension 0
- weight_grad: float32 [8, 1024, 256], P('groups', 'tm'), parts along dimension 0
- cost: float32 [8], P('groups'), parts along dimension 0
There are 2 independent parts, one for each index of `groups`. A program takes and returns all parts, laid end to end along the dimension named above; an argument that names none is the same for every part. Nothing has to cross between parts.
Inputs may be any that keep to these rules, and one draw needn't show every extreme that they name: `links`: each pair names two different blocks, the row before the column, and no pair twice. The lengths of a scenario sum to 1024, and the longest is exactly 512. `decay`: every entry lies strictly between 0 and 1.
All inputs are finite; a program needn't handle non-finite values.
Results may differ from a plain program's by a relative error of at most 0.0003.
Values sent between devices are 32-bit elements; how exact they have to be, the bound alone decides.
No kernel may reach another device: no remote copies, remote signals or barrier semaphores. Data moves between devices by JAX's collectives and lax.ppermute only.
A program may use at most 64 MiB of HBM per device.

v0:
```python
import jax
import jax.numpy as jnp
from jax import lax
from jax.sharding import PartitionSpec as P


def build_dynamics(decay, coupling, links):
    size = decay.shape[0]
    width = coupling.shape[1]
    lanes = jnp.arange(size, dtype=jnp.int32)
    offsets = jnp.arange(width, dtype=jnp.int32)
    row_hot = (lanes[None, :, None] == links[:, 0:1, None] * width + offsets[None, None, :]).astype(
        jnp.float32
    )
    col_hot = (lanes[None, :, None] == links[:, 1:2, None] * width + offsets[None, None, :]).astype(
        jnp.float32
    )
    placed = jnp.einsum(
        "lia,lab,ljb->ij", row_hot, coupling, col_hot, precision=lax.Precision.HIGHEST
    )
    return jnp.diag(decay) + placed


def row_times(values, matrix):
    width = values.shape[-1]
    flat = jnp.dot(values.reshape(-1, width), matrix, precision=lax.Precision.HIGHEST)
    return flat.reshape(values.shape)


def run_chain(inputs, frame_starts, powers, backward, local_levels, device_levels, extra=None):
    scen_count, seg_steps, width = inputs.shape
    devices = lax.axis_size("tm")
    device = lax.axis_index("tm")
    if backward:
        driven = inputs[:, ::-1]
        frame_device = devices - 1 - device
    else:
        driven = inputs
        frame_device = device
    positions = frame_device * seg_steps + jnp.arange(seg_steps, dtype=jnp.int32)
    cut_here = jnp.any(positions[None, :, None] == frame_starts[:, None, :], axis=-1)
    values = driven
    flags = 1.0 - cut_here.astype(jnp.float32)
    for level in range(local_levels):
        stride = 2**level
        prior_values = jnp.pad(values[:, : seg_steps - stride], ((0, 0), (stride, 0), (0, 0)))
        prior_flags = jnp.pad(
            flags[:, : seg_steps - stride], ((0, 0), (stride, 0)), constant_values=1.0
        )
        values = values + flags[:, :, None] * row_times(prior_values, powers[level])
        flags = flags * prior_flags
    last_value = values[:, -1]
    if extra is None:
        all_values = lax.all_gather(last_value[None], "tm", axis=0, tiled=True)
        gathered_extra = None
    else:
        lanes = jnp.broadcast_to(extra[:, None], (scen_count, 128))
        packed = jnp.concatenate([last_value, lanes], axis=1)
        gathered = lax.all_gather(packed[None], "tm", axis=0, tiled=True)
        all_values = gathered[:, :, :width]
        gathered_extra = gathered[:, :, width]
    seg_lo = jnp.arange(devices, dtype=jnp.int32)[:, None, None] * seg_steps
    inside = (frame_starts[None] >= seg_lo) & (frame_starts[None] < seg_lo + seg_steps)
    all_flags = 1.0 - jnp.any(inside, axis=-1).astype(jnp.float32)
    if backward:
        all_values = all_values[::-1]
    roll_by = devices - frame_device
    all_values = jnp.roll(all_values, roll_by, axis=0)
    all_flags = jnp.roll(all_flags, roll_by, axis=0)
    keep = (jnp.arange(devices, dtype=jnp.int32) >= roll_by).astype(jnp.float32)
    all_values = all_values * keep[:, None, None]
    all_flags = all_flags * keep[:, None] + (1.0 - keep[:, None])
    for level in range(device_levels):
        half = all_values.shape[0] // 2
        paired_values = all_values.reshape(half, 2, scen_count, width)
        paired_flags = all_flags.reshape(half, 2, scen_count)
        moved = row_times(paired_values[:, 0], powers[local_levels + level])
        all_values = paired_flags[:, 1, :, None] * moved + paired_values[:, 1]
        all_flags = paired_flags[:, 0] * paired_flags[:, 1]
    entering = all_values[0]
    table = row_times(entering[:, None, :], powers[0])
    for level in range(local_levels):
        table = jnp.concatenate([table, row_times(table, powers[level])], axis=1)
    result = values + flags[:, :, None] * table
    if backward:
        result = result[:, ::-1]
    if extra is None:
        return result
    return (result, gathered_extra)


def per_device(ref_traj, cost_weights, x_init, decay, coupling, links, input_map, ff_gain, lengths):
    scen_count, seg_steps, width = ref_traj.shape
    devices = lax.axis_size("tm")
    device = lax.axis_index("tm")
    total = seg_steps * devices
    high = lax.Precision.HIGHEST
    dynamics = build_dynamics(decay, coupling, links)
    local_levels = seg_steps.bit_length() - 1
    device_levels = (devices - 1).bit_length()
    power_count = local_levels + max(device_levels, 1)
    squares = [dynamics]
    for level in range(power_count - 1):
        squares.append(jnp.dot(squares[-1], squares[-1], precision=high))
    forward_powers = [matrix.T for matrix in squares]
    ends_incl = jnp.cumsum(lengths, axis=1)
    starts = ends_incl - lengths
    mirrored = total - ends_incl
    value_term = run_chain(
        cost_weights * ref_traj, mirrored, squares, True, local_levels, device_levels
    )
    controls = jnp.einsum("stn,cn->stc", value_term, ff_gain, precision=high)
    forcing = -jnp.einsum("stc,nc->stn", controls, input_map, precision=high)
    positions = device * seg_steps + jnp.arange(seg_steps, dtype=jnp.int32)
    start_flag = jnp.any(positions[None, :, None] == starts[:, None, :], axis=-1).astype(
        jnp.float32
    )
    init_image = jnp.dot(x_init, dynamics.T, precision=high)
    driven = forcing + start_flag[:, :, None] * init_image[:, None, :]
    states = run_chain(driven, starts, forward_powers, False, local_levels, device_levels)
    offset = states - ref_traj
    local_cost = jnp.sum(cost_weights * offset * offset, axis=(1, 2)) * (0.5 / total)
    adjoint, all_costs = run_chain(
        cost_weights * offset, mirrored, squares, True, local_levels, device_levels, local_cost
    )
    cost = jnp.sum(all_costs, axis=0)
    pulled = jnp.einsum("stn,nc->stc", adjoint, input_map, precision=high)
    source = -jnp.einsum("stc,cn->stn", pulled, ff_gain, precision=high)
    value_adjoint = run_chain(source, starts, forward_powers, False, local_levels, device_levels)
    weight_grad = 0.5 * offset * offset + ref_traj * value_adjoint
    return (states, weight_grad, cost)


def solution(mesh):
    placed = (
        P("groups", "tm", None),
        P("groups", "tm", None),
        P("groups", None),
        P(),
        P(),
        P(),
        P(),
        P(),
        P("groups", None),
    )
    return jax.shard_map(
        per_device,
        mesh=mesh,
        in_specs=placed,
        out_specs=(P("groups", "tm", None), P("groups", "tm", None), P("groups")),
        check_vma=False,
    )
```

profile of v0, /device:TPU:0, one launch (start us, length us, event | category | flops | bytes accessed | tf_op | source)
XLA Modules:
  0.0 165.5 jit_solution(11104437400287315871)
XLA Ops:
  11.7 0.9 convolution_bitcast_fusion.2
  16.8 0.8 rev.18
  17.6 0.8 slice.315
  18.5 1.3 fusion.23
  22.0 23.4 %all-gather = f32[64,1,256]{2,1,0:T(1,128)S(1)} all-gather(f32[4,1,256]{2,1,0:T(1,128)S(1)} %slice.418), channel_id=2, replica_groups=mesh['groups'=2,'tm'=16] {'tm'}, dimensions={0}, use_global_device_ids=true | all-gather | bytes 69632 | tf_op jit(solution)/shard_map/all_gather | solution.py:54
  49.0 0.9 fusion.68
  50.0 2.5 %concatenate.106 = f32[4,64,256]{2,1,0:T(8,128)S(1)} concatenate(f32[4,1,256]{2,1,0:T(1,128)} %copy-done.14, f32[4,1,256]{2,1,0:T(1,128)} %copy-done.16, f32[4,2,256]{2,1,0:T(2,128)} %copy-done.12, f32[4,4,256]{2,1,0:T(4,128)S(1)} %fusion.104, f32[4,8,256]{2,1,0:T(8,128)S(1)} %fusion.92, f32[4,16,256]{2,1,0:T(8,128)} %copy-done.6, f32[4,32,256]{2,1,0:T(8,128)} %fusion.68), dimensions={1} | concatenate | bytes 524288 | tf_op jit(solution)/shard_map/concatenate | solution.py:83
  52.5 1.5 multiply_add_fusion.2
  54.0 1.0 rev.20
  61.6 17.6 %all-gather.1 = f32[64,1,256]{2,1,0:T(1,128)S(1)} all-gather(f32[4,1,256]{2,1,0:T(1,128)S(1)} %slice.439), channel_id=3, replica_groups=mesh['groups'=2,'tm'=16] {'tm'}, dimensions={0}, use_global_device_ids=true | all-gather | bytes 69632 | tf_op jit(solution)/shard_map/all_gather | solution.py:54
  86.0 1.1 fusion.65
  87.0 3.5 %concatenate.112 = f32[4,64,256]{2,1,0:T(8,128)} concatenate(f32[4,1,256]{2,1,0:T(1,128)S(1)} %reshape.543, f32[4,1,256]{2,1,0:T(1,128)S(1)} %reshape.544, f32[4,2,256]{2,1,0:T(2,128)S(1)} %copy.274, f32[4,4,256]{2,1,0:T(4,128)S(1)} %fusion.101, f32[4,8,256]{2,1,0:T(8,128)S(1)} %fusion.89, f32[4,16,256]{2,1,0:T(8,128)S(1)} %fusion.77, f32[4,32,256]{2,1,0:T(8,128)} %fusion.65), dimensions={1} | concatenate | bytes 524288 | tf_op jit(solution)/shard_map/concatenate | solution.py:83
  90.5 1.9 %multiply_reduce_fusion = (f32[4]{0:T(128)S(1)}, f32[4,64,256]{2,1,0:T(8,128)S(1)}, f32[4,64,256]{2,1,0:T(8,128)}, f32[4,64,256]{2,1,0:T(8,128)}) fusion(f32[4,64,256]{2,1,0:T(8,128)} %param.14, f32[4,64,256]{2,1,0:T(8,128)S(1)} %copy-done.1, f32[4,64,256]{2,1,0:T(8,128)S(1)} %fusion.12, f32[4,64,256]{2,1,0:T(8,128)} %concatenate.112, f32[4,64]{1,0:T(4,128)S(1)} %copy-done.48), kind=kLoop, calls=%fused_computation.176 | loop fusion | flops 393212 | bytes 1836048 | tf_op jit(solution)/shard_map/reduce_sum | solution.py:122
  92.6 0.8 rev.21
  93.3 0.8 slice.374
  94.3 1.3 fusion.11
  99.9 19.2 %all-gather.4 = f32[16,4,384]{2,1,0:T(4,128)S(1)} all-gather(f32[1,4,384]{2,1,0:T(4,128)S(1)} %maximum_bitcast_fusion), channel_id=4, replica_groups=mesh['groups'=2,'tm'=16] {'tm'}, dimensions={0}, use_global_device_ids=true | all-gather | bytes 104448 | tf_op jit(solution)/shard_map/all_gather | solution.py:59
  126.3 0.9 fusion.62
  127.2 2.5 %concatenate.119 = f32[4,64,256]{2,1,0:T(8,128)S(1)} concatenate(f32[4,1,256]{2,1,0:T(1,128)} %copy-done.15, f32[4,1,256]{2,1,0:T(1,128)} %copy-done.17, f32[4,2,256]{2,1,0:T(2,128)} %copy-done.13, f32[4,4,256]{2,1,0:T(4,128)S(1)} %fusion.98, f32[4,8,256]{2,1,0:T(8,128)S(1)} %fusion.86, f32[4,16,256]{2,1,0:T(8,128)} %copy-done.7, f32[4,32,256]{2,1,0:T(8,128)} %fusion.62), dimensions={1} | concatenate | bytes 524288 | tf_op jit(solution)/shard_map/concatenate | solution.py:83
  129.7 1.5 multiply_add_fusion
  131.2 1.0 rev.23
  138.8 17.7 %all-gather.3 = f32[64,1,256]{2,1,0:T(1,128)S(1)} all-gather(f32[4,1,256]{2,1,0:T(1,128)S(1)} %slice.470), channel_id=5, replica_groups=mesh['groups'=2,'tm'=16] {'tm'}, dimensions={0}, use_global_device_ids=true | all-gather | bytes 69632 | tf_op jit(solution)/shard_map/all_gather | solution.py:54
  163.8 0.9 copy-done.3
  164.7 0.8 fusion.46
  (355 shorter events, 58.6 us)
Async XLA Ops:
  0.6 9.7 %copy-start = (f32[3,64,64]{2,1,0:T(8,128)S(1)}, f32[3,64,64]{2,1,0:T(8,128)}, u32[]{:S(2)}) copy-start(f32[3,64,64]{2,1,0:T(8,128)} %param.17) | copy-start | bytes 147460
  0.7 44.9 %copy-start.68 = (f32[16]{0:T(128)}, f32[16]{0:T(128)S(1)}, u32[]{:S(2)}) copy-start(f32[16]{0:T(128)S(1)} %compare_convert_fusion.1) | copy-start | bytes 196
  0.8 6.6 %copy-start.65 = (f32[16]{0:T(128)}, f32[16]{0:T(128)S(1)}, u32[]{:S(2)}) copy-start(f32[16]{0:T(128)S(1)} %compare_convert_fusion) | copy-start | bytes 196
  2.5 15.8 %copy-start.46 = (f32[4,64]{1,0:T(4,128)}, f32[4,64]{1,0:T(4,128)S(1)}, u32[]{:S(2)}) copy-start(f32[4,64]{1,0:T(4,128)S(1)} %convert_subtract_fusion.2) | copy-start | bytes 3076
  2.6 17.2 %copy-start.41 = (f32[4,64]{1,0:T(4,128)}, f32[4,64]{1,0:T(4,128)S(1)}, u32[]{:S(2)}) copy-start(f32[4,64]{1,0:T(4,128)S(1)} %pad_multiply_fusion.11) | copy-start | bytes 3076
  2.7 17.6 %copy-start.39 = (f32[4,64]{1,0:T(4,128)}, f32[4,64]{1,0:T(4,128)S(1)}, u32[]{:S(2)}) copy-start(f32[4,64]{1,0:T(4,128)S(1)} %pad_multiply_fusion.10) | copy-start | bytes 3076
  2.8 17.9 %copy-start.37 = (f32[4,64]{1,0:T(4,128)}, f32[4,64]{1,0:T(4,128)S(1)}, u32[]{:S(2)}) copy-start(f32[4,64]{1,0:T(4,128)S(1)} %pad_multiply_fusion.9) | copy-start | bytes 3076
  2.9 18.3 %copy-start.35 = (f32[4,64]{1,0:T(4,128)}, f32[4,64]{1,0:T(4,128)S(1)}, u32[]{:S(2)}) copy-start(f32[4,64]{1,0:T(4,128)S(1)} %pad_multiply_fusion.8) | copy-start | bytes 3076
  2.9 18.6 %copy-start.33 = (f32[4,64]{1,0:T(4,128)}, f32[4,64]{1,0:T(4,128)S(1)}, u32[]{:S(2)}) copy-start(f32[4,64]{1,0:T(4,128)S(1)} %pad_multiply_fusion.7) | copy-start | bytes 3076
  7.8 38.2 %copy-start.56 = (f32[4,1,4]{2,1,0:T(1,128)}, f32[4,1,4]{2,1,0:T(1,128)S(1)}, u32[]{:S(2)}) copy-start(f32[4,1,4]{2,1,0:T(1,128)S(1)} %get-tuple-element.34) | copy-start | bytes 196
  7.8 38.5 %copy-start.61 = (f32[2,1,4]{2,1,0:T(1,128)}, f32[2,1,4]{2,1,0:T(1,128)S(1)}, u32[]{:S(2)}) copy-start(f32[2,1,4]{2,1,0:T(1,128)S(1)} %get-tuple-element.38) | copy-start | bytes 100
  7.8 38.7 %copy-start.73 = (f32[4]{0:T(128)}, f32[4]{0:T(128)S(1)}, u32[]{:S(2)}) copy-start(f32[4]{0:T(128)S(1)} %slice_bitcast_fusion.25) | copy-start | bytes 52
  7.9 37.8 %copy-start.52 = (f32[8,1,4]{0,2,1:T(4,128)}, f32[8,1,4]{0,2,1:T(4,128)S(1)}, u32[]{:S(2)}) copy-start(f32[8,1,4]{0,2,1:T(4,128)S(1)} %copy.244) | copy-start | bytes 388
  15.7 1.0 copy-start.1
  15.7 1.0 copy-start.2
  47.0 1.4 copy-start.14
  47.3 1.1 copy-start.16
  54.0 1.0 copy-start.10
  87.0 3.5 %copy-start.48 = (f32[4,64]{1,0:T(4,128)S(1)}, f32[4,64]{1,0:T(4,128)}, u32[]{:S(2)}) copy-start(f32[4,64]{1,0:T(4,128)} %pad_multiply_fusion) | copy-start | bytes 3076
  94.3 1.4 copy-start.42
  124.3 1.4 copy-start.15
  124.5 1.1 copy-start.17
  131.2 1.0 copy-start.9
  163.7 1.0 copy-start.3
  (53 other events, 37.1 us)
where the time goes:
time: 167 us; the launch traced here: 165 us
  blocking collectives  78 us (47%)
  local copies, waits for them, and re-layouts  40.9 us (24%)
  matrix products  32.3 us (19%)
  other arithmetic  12 us (7%)
  between operations  2.32 us (1%)
    all_gather x3, blocking collectives, run_chain(): all_values = lax.all_gather(last_value[None], 'tm', axis=0, tiled=True)  58.7 us
    dot_general x68, matrix products, row_times(): jnp.dot(values.reshape(-1, width), matrix, precision=lax.Precision.HIGHEST)  25.8 us
    unnamed x155, local copies, waits for them, and re-layouts  24.6 us
    all_gather x1, blocking collectives, run_chain(): gathered = lax.all_gather(packed[None], 'tm', axis=0, tiled=True)  19.2 us
    concatenate x12, local copies, waits for them, and re-layouts, run_chain(): table = jnp.concatenate([table, row_times(table, powers[level])], axis=1)  8.84 us
    dot_general x9, matrix products, per_device(): squares.append(jnp.dot(squares[-1], squares[-1], precision=high))  3.4 us

commit v1 on v0

--- a/solution.py
+++ b/solution.py
@@ -2,6 +2,12 @@
 import jax.numpy as jnp
 from jax import lax
 from jax.sharding import PartitionSpec as P
+
+
+def joined_along(blocks, dim):
+    shape = list(blocks.shape[1:])
+    shape[dim] *= blocks.shape[0]
+    return jnp.moveaxis(blocks, 0, dim).reshape(shape)
 
 
 def build_dynamics(decay, coupling, links):
@@ -56,7 +62,19 @@
     else:
         lanes = jnp.broadcast_to(extra[:, None], (scen_count, 128))
         packed = jnp.concatenate([last_value, lanes], axis=1)
-        gathered = lax.all_gather(packed[None], "tm", axis=0, tiled=True)
+        size_2 = lax.axis_size("tm")
+        pairs = [(i, (i + 1) % size_2) for i in range(size_2)]
+        back = [(b, a) for a, b in pairs]
+        lower, upper = ([], [])
+        for step in range(size_2 - 1):
+            if step % 2 == 0:
+                lower.append(lax.ppermute(lower[-1] if lower else packed[None], "tm", pairs))
+            else:
+                upper.append(lax.ppermute(upper[-1] if upper else packed[None], "tm", back))
+        tiles = jnp.stack([*lower[::-1], packed[None], *upper])
+        shift = lax.axis_index("tm") - len(lower)
+        tiles = tiles[(jnp.arange(size_2) - shift) % size_2]
+        gathered = joined_along(tiles, 0)
         all_values = gathered[:, :, :width]
         gathered_extra = gathered[:, :, width]
     seg_lo = jnp.arange(devices, dtype=jnp.int32)[:, None, None] * seg_steps

time: 167 us -> 184 us (1.10)
  starting transfers between devices: 0 us -> 31.3 us
  blocking collectives: 78 us -> 59.1 us
  waiting for transfers between devices: 0 us -> 14.7 us
  local copies, waits for them, and re-layouts: 40.9 us -> 31.8 us
  matrix products: 32.3 us -> 30.1 us
    ppermute x0 -> x15, starting transfers between devices: none -> 31.3 us  [the longest x7 30.9 us: run_chain(): upper.append(lax.ppermute(upper[-1] if upper else packed[None], 'tm', back))]
    all_gather x1 -> x0, blocking collectives: 19.2 us -> none  [run_chain(): gathered = lax.all_gather(packed[None], 'tm', axis=0, tiled=True)]
    ppermute x0 -> x15, waiting for transfers between devices: none -> 14.7 us  [the longest x8 14.4 us: run_chain(): lax.ppermute(lower[-1] if lower else packed[None], 'tm', pairs)]
    unnamed x155 -> x131, local copies, waits for them, and re-layouts: 24.6 us -> 19.8 us
    concatenate x12, local copies, waits for them, and re-layouts: 8.84 us -> 5.49 us  [run_chain(): table = jnp.concatenate([table, row_times(table, powers[level])], axis=1)]
    dot_general x68, matrix products: 25.8 us -> 23.6 us  [row_times(): jnp.dot(values.reshape(-1, width), matrix, precision=lax.Precision.HIGHEST)]
  transfers between devices with their start and end apart: 0 -> 15, of which waited for: 0 -> 9; matrix products, arithmetic and copies ran while one was open for 0% -> 0% of each run, Pallas kernels for 0% -> 0%
where the time goes in v1:
time: 184 us; the launch traced here: 183 us
  blocking collectives  59.1 us (32%)
  local copies, waits for them, and re-layouts  31.8 us (17%)
  starting transfers between devices  31.3 us (17%)
  matrix products  30.1 us (16%)
  waiting for transfers between devices  14.7 us (8%)
  other arithmetic  13.4 us (7%)
  between operations  2.21 us (1%)
    all_gather x3, blocking collectives, run_chain(): all_values = lax.all_gather(last_value[None], 'tm', axis=0, tiled=True)  59.1 us
    ppermute x7, starting transfers between devices, run_chain(): upper.append(lax.ppermute(upper[-1] if upper else packed[None], 'tm', back))  30.9 us
    dot_general x68, matrix products, row_times(): jnp.dot(values.reshape(-1, width), matrix, precision=lax.Precision.HIGHEST)  23.6 us
    unnamed x131, local copies, waits for them, and re-layouts  19.8 us
    ppermute x8, waiting for transfers between devices, run_chain(): lax.ppermute(lower[-1] if lower else packed[None], 'tm', pairs)  14.4 us
    concatenate x12, local copies, waits for them, and re-layouts, run_chain(): table = jnp.concatenate([table, row_times(table, powers[level])], axis=1)  5.49 us
  transfers between devices with their start and end apart: 15, of which 9 were waited for; matrix products, arithmetic and copies ran while one was open for 0% of the time, Pallas kernels for 0%

profile of v1, /device:TPU:0, one launch (start us, length us, event | category | flops | bytes accessed | tf_op | source)
XLA Modules:
  0.0 182.5 jit_solution(8503031377254725047)
XLA Ops:
  3.8 1.1 mul.581
  15.4 23.4 %all-gather = f32[64,1,256]{2,1,0:T(1,128)S(1)} all-gather(f32[4,1,256]{2,1,0:T(1,128)S(1)} %slice.420), channel_id=2, replica_groups=mesh['groups'=2,'tm'=16] {'tm'}, dimensions={0}, use_global_device_ids=true | all-gather | bytes 69632 | tf_op jit(solution)/shard_map/all_gather | solution.py:60
  54.6 17.6 %all-gather.1 = f32[64,1,256]{2,1,0:T(1,128)S(1)} all-gather(f32[4,1,256]{2,1,0:T(1,128)S(1)} %slice.441), channel_id=3, replica_groups=mesh['groups'=2,'tm'=16] {'tm'}, dimensions={0}, use_global_device_ids=true | all-gather | bytes 69632 | tf_op jit(solution)/shard_map/all_gather | solution.py:60
  79.3 2.6 %concatenate.112 = f32[4,64,256]{2,1,0:T(8,128)} concatenate(f32[4,1,256]{2,1,0:T(1,128)S(1)} %reshape.595, f32[4,1,256]{2,1,0:T(1,128)S(1)} %reshape.596, f32[4,2,256]{2,1,0:T(2,128)S(1)} %copy.217, f32[4,4,256]{2,1,0:T(4,128)S(1)} %fusion.101, f32[4,8,256]{2,1,0:T(8,128)S(1)} %fusion.89, f32[4,16,256]{2,1,0:T(8,128)S(1)} %fusion.77, f32[4,32,256]{2,1,0:T(8,128)S(1)} %fusion.65), dimensions={1} | concatenate | bytes 524288 | tf_op jit(solution)/shard_map/concatenate | solution.py:101
  81.9 1.9 %multiply_reduce_fusion = (f32[4]{0:T(128)S(1)}, f32[4,64,256]{2,1,0:T(8,128)S(1)}, f32[4,64,256]{2,1,0:T(8,128)}, f32[4,64,256]{2,1,0:T(8,128)}) fusion(f32[4,64,256]{2,1,0:T(8,128)} %param.14, f32[4,64,256]{2,1,0:T(8,128)S(1)} %copy-done.1, f32[4,64,256]{2,1,0:T(8,128)S(1)} %fusion.12, f32[4,64,256]{2,1,0:T(8,128)} %concatenate.112, ...), kind=kLoop, calls=%fused_computation.177 | loop fusion | flops 393212 | bytes 1836048 | tf_op jit(solution)/shard_map/reduce_sum | solution.py:140
  85.6 1.3 fusion.11
  89.4 5.4 %collective-permute-done = f32[1,4,384]{2,1,0:T(4,128)S(1)} collective-permute-done((f32[1,4,384]{2,1,0:T(4,128)S(1)}, f32[1,4,384]{2,1,0:T(4,128)S(1)}, u32[]{:S(2)}, u32[]{:S(2)}) %collective-permute-start) | collective-permute-done | bytes 6176 | tf_op jit(solution)/shard_map/ppermute | solution.py:71
  94.8 4.4 %collective-permute-start.8 = (f32[1,4,384]{2,1,0:T(4,128)S(1)}, f32[1,4,384]{2,1,0:T(4,128)S(1)}, u32[]{:S(2)}, u32[]{:S(2)}) collective-permute-start(f32[1,4,384]{2,1,0:T(4,128)S(1)} %fusion.199), channel_id=1, source_target_pairs={{1,0},{2,1},{3,2},{4,3},{5,4},{6,5},{7,6},{8,7},{9,8},{10,9},{11,1... | collective-permute-start | bytes 18440 | tf_op jit(solution)/shard_map/ppermute | solution.py:73
  99.3 1.3 collective-permute-done.1
  100.6 4.4 %collective-permute-start.9 = (f32[1,4,384]{2,1,0:T(4,128)S(1)}, f32[1,4,384]{2,1,0:T(4,128)S(1)}, u32[]{:S(2)}, u32[]{:S(2)}) collective-permute-start(f32[1,4,384]{2,1,0:T(4,128)S(1)} %collective-permute-done.8), channel_id=1, source_target_pairs={{1,0},{2,1},{3,2},{4,3},{5,4},{6,5},{7,6},{8,7},{9,8},{10,9},{11,1... | collective-permute-start | bytes 18440 | tf_op jit(solution)/shard_map/ppermute | solution.py:73
  105.0 1.3 collective-permute-done.2
  106.4 4.4 %collective-permute-start.10 = (f32[1,4,384]{2,1,0:T(4,128)S(1)}, f32[1,4,384]{2,1,0:T(4,128)S(1)}, u32[]{:S(2)}, u32[]{:S(2)}) collective-permute-start(f32[1,4,384]{2,1,0:T(4,128)S(1)} %collective-permute-done.9), channel_id=1, source_target_pairs={{1,0},{2,1},{3,2},{4,3},{5,4},{6,5},{7,6},{8,7},{9,8},{10,9},{11,1... | collective-permute-start | bytes 18440 | tf_op jit(solution)/shard_map/ppermute | solution.py:73
  110.8 1.3 collective-permute-done.3
  112.1 4.4 %collective-permute-start.11 = (f32[1,4,384]{2,1,0:T(4,128)S(1)}, f32[1,4,384]{2,1,0:T(4,128)S(1)}, u32[]{:S(2)}, u32[]{:S(2)}) collective-permute-start(f32[1,4,384]{2,1,0:T(4,128)S(1)} %collective-permute-done.10), channel_id=1, source_target_pairs={{1,0},{2,1},{3,2},{4,3},{5,4},{6,5},{7,6},{8,7},{9,8},{10,9},{11,1... | collective-permute-start | bytes 18440 | tf_op jit(solution)/shard_map/ppermute | solution.py:73
  116.5 1.3 collective-permute-done.4
  117.9 4.4 %collective-permute-start.12 = (f32[1,4,384]{2,1,0:T(4,128)S(1)}, f32[1,4,384]{2,1,0:T(4,128)S(1)}, u32[]{:S(2)}, u32[]{:S(2)}) collective-permute-start(f32[1,4,384]{2,1,0:T(4,128)S(1)} %collective-permute-done.11), channel_id=1, source_target_pairs={{1,0},{2,1},{3,2},{4,3},{5,4},{6,5},{7,6},{8,7},{9,8},{10,9},{11,1... | collective-permute-start | bytes 18440 | tf_op jit(solution)/shard_map/ppermute | solution.py:73
  122.3 1.3 collective-permute-done.5
  123.6 4.5 %collective-permute-start.13 = (f32[1,4,384]{2,1,0:T(4,128)S(1)}, f32[1,4,384]{2,1,0:T(4,128)S(1)}, u32[]{:S(2)}, u32[]{:S(2)}) collective-permute-start(f32[1,4,384]{2,1,0:T(4,128)S(1)} %collective-permute-done.12), channel_id=1, source_target_pairs={{1,0},{2,1},{3,2},{4,3},{5,4},{6,5},{7,6},{8,7},{9,8},{10,9},{11,1... | collective-permute-start | bytes 18440 | tf_op jit(solution)/shard_map/ppermute | solution.py:73
  128.1 1.2 collective-permute-done.6
  129.5 4.4 %collective-permute-start.14 = (f32[1,4,384]{2,1,0:T(4,128)S(1)}, f32[1,4,384]{2,1,0:T(4,128)S(1)}, u32[]{:S(2)}, u32[]{:S(2)}) collective-permute-start(f32[1,4,384]{2,1,0:T(4,128)S(1)} %collective-permute-done.13), channel_id=1, source_target_pairs={{1,0},{2,1},{3,2},{4,3},{5,4},{6,5},{7,6},{8,7},{9,8},{10,9},{11,1... | collective-permute-start | bytes 18440 | tf_op jit(solution)/shard_map/ppermute | solution.py:73
  133.9 1.2 collective-permute-done.7
  144.0 2.5 %concatenate.119 = f32[4,64,256]{2,1,0:T(8,128)S(1)} concatenate(f32[4,1,256]{2,1,0:T(1,128)} %copy-done.10, f32[4,1,256]{2,1,0:T(1,128)} %copy-done.11, f32[4,2,256]{2,1,0:T(2,128)} %copy-done.9, f32[4,4,256]{2,1,0:T(4,128)S(1)} %fusion.98, f32[4,8,256]{2,1,0:T(8,128)S(1)} %fusion.86, f32[4,16,256]{2,1,0:T(8,128)} %copy-done.4, f32[4,32,256]{2,1,0:T(8,128)} %fusion.62), dimensions={1} | concatenate | bytes 524288 | tf_op jit(solution)/shard_map/concatenate | solution.py:101
  146.5 1.5 multiply_add_fusion
  155.6 18.1 %all-gather.2 = f32[64,1,256]{2,1,0:T(1,128)S(1)} all-gather(f32[4,1,256]{2,1,0:T(1,128)S(1)} %slice.472), channel_id=4, replica_groups=mesh['groups'=2,'tm'=16] {'tm'}, dimensions={0}, use_global_device_ids=true | all-gather | bytes 69632 | tf_op jit(solution)/shard_map/all_gather | solution.py:60
  (365 shorter events, 65.0 us)
Async XLA Ops:
  3.2 48.7 %copy-start.22 = (f32[4,64]{1,0:T(4,128)}, f32[4,64]{1,0:T(4,128)S(1)}, u32[]{:S(2)}) copy-start(f32[4,64]{1,0:T(4,128)S(1)} %broadcast_subtract_fusion.1) | copy-start | bytes 3076
  7.1 33.0 %copy-start.30 = (f32[4,1,4]{2,1,0:T(1,128)}, f32[4,1,4]{2,1,0:T(1,128)S(1)}, u32[]{:S(2)}) copy-start(f32[4,1,4]{2,1,0:T(1,128)S(1)} %get-tuple-element.34) | copy-start | bytes 196
  7.1 33.3 %copy-start.35 = (f32[2,1,4]{2,1,0:T(1,128)}, f32[2,1,4]{2,1,0:T(1,128)S(1)}, u32[]{:S(2)}) copy-start(f32[2,1,4]{2,1,0:T(1,128)S(1)} %get-tuple-element.38) | copy-start | bytes 100
  7.8 32.0 %copy-start.24 = (f32[8,1,4]{0,2,1:T(4,128)}, f32[8,1,4]{0,2,1:T(4,128)S(1)}, u32[]{:S(2)}) copy-start(f32[8,1,4]{0,2,1:T(4,128)S(1)} %copy.187) | copy-start | bytes 388
  42.5 9.8 %copy-start.20 = (f32[4,64]{1,0:T(4,128)}, f32[4,64]{1,0:T(4,128)S(1)}, u32[]{:S(2)}) copy-start(f32[4,64]{1,0:T(4,128)S(1)} %pad_multiply_fusion.5) | copy-start | bytes 3076
  42.6 10.2 %copy-start.18 = (f32[4,64]{1,0:T(4,128)}, f32[4,64]{1,0:T(4,128)S(1)}, u32[]{:S(2)}) copy-start(f32[4,64]{1,0:T(4,128)S(1)} %pad_multiply_fusion.4) | copy-start | bytes 3076
  42.7 10.6 %copy-start.16 = (f32[4,64]{1,0:T(4,128)}, f32[4,64]{1,0:T(4,128)S(1)}, u32[]{:S(2)}) copy-start(f32[4,64]{1,0:T(4,128)S(1)} %pad_multiply_fusion.3) | copy-start | bytes 3076
  42.7 11.0 %copy-start.14 = (f32[4,64]{1,0:T(4,128)}, f32[4,64]{1,0:T(4,128)S(1)}, u32[]{:S(2)}) copy-start(f32[4,64]{1,0:T(4,128)S(1)} %pad_multiply_fusion.2) | copy-start | bytes 3076
  42.8 34.5 %copy-start.12 = (f32[4,64]{1,0:T(4,128)}, f32[4,64]{1,0:T(4,128)S(1)}, u32[]{:S(2)}) copy-start(f32[4,64]{1,0:T(4,128)S(1)} %pad_multiply_fusion.1) | copy-start | bytes 3076
  89.1 5.8 %collective-permute-start = (f32[1,4,384]{2,1,0:T(4,128)S(1)}, f32[1,4,384]{2,1,0:T(4,128)S(1)}, u32[]{:S(2)}, u32[]{:S(2)}) collective-permute-start(f32[1,4,384]{2,1,0:T(4,128)S(1)} %fusion.199), channel_id=1, source_target_pairs={{0,1},{1,2},{2,3},{3,4},{4,5},{5,6},{6,7},{7,8},{8,9},{9,10},{10,1... | collective-permute-start | bytes 18440 | tf_op jit(solution)/shard_map/ppermute | solution.py:71
  94.8 5.8 %collective-permute-start.1 = (f32[1,4,384]{2,1,0:T(4,128)S(1)}, f32[1,4,384]{2,1,0:T(4,128)S(1)}, u32[]{:S(2)}, u32[]{:S(2)}) collective-permute-start(f32[1,4,384]{2,1,0:T(4,128)S(1)} %collective-permute-done), channel_id=1, source_target_pairs={{0,1},{1,2},{2,3},{3,4},{4,5},{5,6},{6,7},{7,8},{8,9},{9,10},{10,1... | collective-permute-start | bytes 18440 | tf_op jit(solution)/shard_map/ppermute | solution.py:71
  94.8 5.8 %collective-permute-start.8 = (f32[1,4,384]{2,1,0:T(4,128)S(1)}, f32[1,4,384]{2,1,0:T(4,128)S(1)}, u32[]{:S(2)}, u32[]{:S(2)}) collective-permute-start(f32[1,4,384]{2,1,0:T(4,128)S(1)} %fusion.199), channel_id=1, source_target_pairs={{1,0},{2,1},{3,2},{4,3},{5,4},{6,5},{7,6},{8,7},{9,8},{10,9},{11,1... | collective-permute-start | bytes 18440 | tf_op jit(solution)/shard_map/ppermute | solution.py:73
  100.6 5.8 %collective-permute-start.2 = (f32[1,4,384]{2,1,0:T(4,128)S(1)}, f32[1,4,384]{2,1,0:T(4,128)S(1)}, u32[]{:S(2)}, u32[]{:S(2)}) collective-permute-start(f32[1,4,384]{2,1,0:T(4,128)S(1)} %collective-permute-done.1), channel_id=1, source_target_pairs={{0,1},{1,2},{2,3},{3,4},{4,5},{5,6},{6,7},{7,8},{8,9},{9,10},{10,1... | collective-permute-start | bytes 18440 | tf_op jit(solution)/shard_map/ppermute | solution.py:71
  100.6 5.8 %collective-permute-start.9 = (f32[1,4,384]{2,1,0:T(4,128)S(1)}, f32[1,4,384]{2,1,0:T(4,128)S(1)}, u32[]{:S(2)}, u32[]{:S(2)}) collective-permute-start(f32[1,4,384]{2,1,0:T(4,128)S(1)} %collective-permute-done.8), channel_id=1, source_target_pairs={{1,0},{2,1},{3,2},{4,3},{5,4},{6,5},{7,6},{8,7},{9,8},{10,9},{11,1... | collective-permute-start | bytes 18440 | tf_op jit(solution)/shard_map/ppermute | solution.py:73
  106.3 5.8 %collective-permute-start.3 = (f32[1,4,384]{2,1,0:T(4,128)S(1)}, f32[1,4,384]{2,1,0:T(4,128)S(1)}, u32[]{:S(2)}, u32[]{:S(2)}) collective-permute-start(f32[1,4,384]{2,1,0:T(4,128)S(1)} %collective-permute-done.2), channel_id=1, source_target_pairs={{0,1},{1,2},{2,3},{3,4},{4,5},{5,6},{6,7},{7,8},{8,9},{9,10},{10,1... | collective-permute-start | bytes 18440 | tf_op jit(solution)/shard_map/ppermute | solution.py:71
  106.4 5.8 %collective-permute-start.10 = (f32[1,4,384]{2,1,0:T(4,128)S(1)}, f32[1,4,384]{2,1,0:T(4,128)S(1)}, u32[]{:S(2)}, u32[]{:S(2)}) collective-permute-start(f32[1,4,384]{2,1,0:T(4,128)S(1)} %collective-permute-done.9), channel_id=1, source_target_pairs={{1,0},{2,1},{3,2},{4,3},{5,4},{6,5},{7,6},{8,7},{9,8},{10,9},{11,1... | collective-permute-start | bytes 18440 | tf_op jit(solution)/shard_map/ppermute | solution.py:73
  112.1 5.8 %collective-permute-start.4 = (f32[1,4,384]{2,1,0:T(4,128)S(1)}, f32[1,4,384]{2,1,0:T(4,128)S(1)}, u32[]{:S(2)}, u32[]{:S(2)}) collective-permute-start(f32[1,4,384]{2,1,0:T(4,128)S(1)} %collective-permute-done.3), channel_id=1, source_target_pairs={{0,1},{1,2},{2,3},{3,4},{4,5},{5,6},{6,7},{7,8},{8,9},{9,10},{10,1... | collective-permute-start | bytes 18440 | tf_op jit(solution)/shard_map/ppermute | solution.py:71
  112.1 5.8 %collective-permute-start.11 = (f32[1,4,384]{2,1,0:T(4,128)S(1)}, f32[1,4,384]{2,1,0:T(4,128)S(1)}, u32[]{:S(2)}, u32[]{:S(2)}) collective-permute-start(f32[1,4,384]{2,1,0:T(4,128)S(1)} %collective-permute-done.10), channel_id=1, source_target_pairs={{1,0},{2,1},{3,2},{4,3},{5,4},{6,5},{7,6},{8,7},{9,8},{10,9},{11,1... | collective-permute-start | bytes 18440 | tf_op jit(solution)/shard_map/ppermute | solution.py:73
  117.8 5.8 %collective-permute-start.5 = (f32[1,4,384]{2,1,0:T(4,128)S(1)}, f32[1,4,384]{2,1,0:T(4,128)S(1)}, u32[]{:S(2)}, u32[]{:S(2)}) collective-permute-start(f32[1,4,384]{2,1,0:T(4,128)S(1)} %collective-permute-done.4), channel_id=1, source_target_pairs={{0,1},{1,2},{2,3},{3,4},{4,5},{5,6},{6,7},{7,8},{8,9},{9,10},{10,1... | collective-permute-start | bytes 18440 | tf_op jit(solution)/shard_map/ppermute | solution.py:71
  117.9 5.8 %collective-permute-start.12 = (f32[1,4,384]{2,1,0:T(4,128)S(1)}, f32[1,4,384]{2,1,0:T(4,128)S(1)}, u32[]{:S(2)}, u32[]{:S(2)}) collective-permute-start(f32[1,4,384]{2,1,0:T(4,128)S(1)} %collective-permute-done.11), channel_id=1, source_target_pairs={{1,0},{2,1},{3,2},{4,3},{5,4},{6,5},{7,6},{8,7},{9,8},{10,9},{11,1... | collective-permute-start | bytes 18440 | tf_op jit(solution)/shard_map/ppermute | solution.py:73
  123.6 5.8 %collective-permute-start.6 = (f32[1,4,384]{2,1,0:T(4,128)S(1)}, f32[1,4,384]{2,1,0:T(4,128)S(1)}, u32[]{:S(2)}, u32[]{:S(2)}) collective-permute-start(f32[1,4,384]{2,1,0:T(4,128)S(1)} %collective-permute-done.5), channel_id=1, source_target_pairs={{0,1},{1,2},{2,3},{3,4},{4,5},{5,6},{6,7},{7,8},{8,9},{9,10},{10,1... | collective-permute-start | bytes 18440 | tf_op jit(solution)/shard_map/ppermute | solution.py:71
  123.6 5.8 %collective-permute-start.13 = (f32[1,4,384]{2,1,0:T(4,128)S(1)}, f32[1,4,384]{2,1,0:T(4,128)S(1)}, u32[]{:S(2)}, u32[]{:S(2)}) collective-permute-start(f32[1,4,384]{2,1,0:T(4,128)S(1)} %collective-permute-done.12), channel_id=1, source_target_pairs={{1,0},{2,1},{3,2},{4,3},{5,4},{6,5},{7,6},{8,7},{9,8},{10,9},{11,1... | collective-permute-start | bytes 18440 | tf_op jit(solution)/shard_map/ppermute | solution.py:73
  129.4 5.8 %collective-permute-start.7 = (f32[1,4,384]{2,1,0:T(4,128)S(1)}, f32[1,4,384]{2,1,0:T(4,128)S(1)}, u32[]{:S(2)}, u32[]{:S(2)}) collective-permute-start(f32[1,4,384]{2,1,0:T(4,128)S(1)} %collective-permute-done.6), channel_id=1, source_target_pairs={{0,1},{1,2},{2,3},{3,4},{4,5},{5,6},{6,7},{7,8},{8,9},{9,10},{10,1... | collective-permute-start | bytes 18440 | tf_op jit(solution)/shard_map/ppermute | solution.py:71
  129.5 5.8 %collective-permute-start.14 = (f32[1,4,384]{2,1,0:T(4,128)S(1)}, f32[1,4,384]{2,1,0:T(4,128)S(1)}, u32[]{:S(2)}, u32[]{:S(2)}) collective-permute-start(f32[1,4,384]{2,1,0:T(4,128)S(1)} %collective-permute-done.13), channel_id=1, source_target_pairs={{1,0},{2,1},{3,2},{4,3},{5,4},{6,5},{7,6},{8,7},{9,8},{10,9},{11,1... | collective-permute-start | bytes 18440 | tf_op jit(solution)/shard_map/ppermute | solution.py:73
  (49 other events, 54.8 us)
